TPU v7x, 512 devices: a whole 4x4x16 slice. The times are simulated.
512 devices in a mesh: ctx: 64 (over x_hi, z, core), head: 8 (over x_lo, y).
Axes of the slice: x: 4 (x_hi: 2, x_lo: 2; x = x_hi * 2 + x_lo), y: 4, z: 16, core: 2. Of those that a mesh axis runs over, the one named last changes fastest.
Arguments:
- q_latent: bfloat16 [8192, 64, 512], P('ctx', 'head'), may hold values from -1.25 to 1.25
- q_rope: bfloat16 [8192, 4096], P('ctx', 'head'), may hold values from -1.25 to 1.25
- attn_out: bfloat16 [8192, 64, 512], P('ctx', 'head'), may hold values from -4 to 4
- grad_out: bfloat16 [8192, 64, 512], P('ctx', 'head'), may hold values from -1 to 1
- log_total: float32 [8192, 64], P('ctx', 'head'), may hold values from 4 to 6
- latent: bfloat16 [8192, 512], P('ctx'), may hold values from -2.5 to 2.5
- key_rope: bfloat16 [8192, 64], P('ctx'), may hold values from -2.5 to 2.5
- doc_start: int32 [8192], P('ctx'), may hold values from 0 to 8191, as said below
Outputs:
- grad_q_latent: bfloat16 [8192, 64, 512], P('ctx', 'head')
- grad_q_rope: bfloat16 [8192, 4096], P('ctx', 'head')
- grad_latent: bfloat16 [8192, 512], P(('ctx', 'head'))
- grad_key_rope: bfloat16 [8192, 64], P(('ctx', 'head'))
Inputs may be any that keep to these rules, and one draw needn't show every extreme that they name: doc_start[t] is the first token of the document that holds token t. Documents are runs of 1 to 897 tokens laid end to end from token 0; one document has exactly 897 tokens, and the last token of the sequence is a document of its own.
All inputs are finite; a program needn't handle non-finite values.
Results may differ from a plain program's by a relative error of at most 0.0056.
Values may be sent and summed in bfloat16 or wider, within the bound.
No kernel may reach another device: no remote copies, remote signals or barrier semaphores. Data moves between devices by JAX's collectives and lax.ppermute only.
A program may use at most 64 MiB of HBM per device.

v0:
```python
import jax
import jax.numpy as jnp
from jax import lax
from jax.sharding import PartitionSpec as P

ROPE = 64
NOPE = 128
LEVELS = 3


def shifted(x, axis, by):
    count = lax.axis_size(axis)
    pairs = [(i, i + by) for i in range(count) if 0 <= i + by < count]
    return lax.ppermute(x, axis, pairs)


def local(q_latent, q_rope, attn_out, grad_out, log_total, latent, key_rope, doc_start):
    tok_rows, head_count, lat_width = q_latent.shape
    rope_width = key_rope.shape[1]
    span = 2**LEVELS
    groups = lax.axis_size("head")
    softmax_scale = (NOPE + ROPE) ** (-0.5)
    q_rot = q_rope.reshape(tok_rows, head_count, rope_width)
    row_delta = jnp.einsum("thc,thc->th", grad_out, attn_out, preferred_element_type=jnp.float32)
    own_tile = lax.axis_index("ctx")
    query_pos = own_tile * tok_rows + jnp.arange(tok_rows, dtype=jnp.int32)
    keys = jnp.concatenate([latent, key_rope], axis=1)[None]
    width = 1
    while width < span:
        keys = jnp.concatenate([shifted(keys, "ctx", width), keys], axis=0)
        width *= 2
    keys = keys.reshape(span * tok_rows, lat_width + rope_width)
    lat_all = keys[:, :lat_width]
    rot_all = keys[:, lat_width:]
    key_pos = (own_tile - span + 1) * tok_rows + jnp.arange(span * tok_rows, dtype=jnp.int32)
    visible = ((key_pos[None, :] >= doc_start[:, None]) & (key_pos[None, :] <= query_pos[:, None]))[
        :, None, :
    ]
    scores = (
        jnp.einsum("thc,kc->thk", q_latent, lat_all, preferred_element_type=jnp.float32)
        + jnp.einsum("thr,kr->thk", q_rot, rot_all, preferred_element_type=jnp.float32)
    ) * softmax_scale
    probs = jnp.where(
        visible, jnp.exp(jnp.where(visible, scores, 0.0) - log_total[:, :, None]), 0.0
    )
    grad_probs = jnp.einsum("thc,kc->thk", grad_out, lat_all, preferred_element_type=jnp.float32)
    grad_scores = probs * (grad_probs - row_delta[:, :, None])
    probs_b = probs.astype(jnp.bfloat16)
    grad_b = grad_scores.astype(jnp.bfloat16)
    grad_qlat = softmax_scale * jnp.einsum(
        "thk,kc->thc", grad_b, lat_all, preferred_element_type=jnp.float32
    )
    grad_qrot = softmax_scale * jnp.einsum(
        "thk,kr->thr", grad_b, rot_all, preferred_element_type=jnp.float32
    )
    grad_lat = softmax_scale * jnp.einsum(
        "thk,thc->kc", grad_b, q_latent, preferred_element_type=jnp.float32
    ) + jnp.einsum("thk,thc->kc", probs_b, grad_out, preferred_element_type=jnp.float32)
    grad_rot = softmax_scale * jnp.einsum(
        "thk,thr->kr", grad_b, q_rot, preferred_element_type=jnp.float32
    )
    part = jnp.concatenate([grad_lat, grad_rot], axis=1)
    block = tok_rows // groups
    part = part.reshape(span, groups, block, lat_width + rope_width)
    part = lax.all_to_all(part, "head", 1, 1, tiled=True).sum(axis=1)
    width = span
    while width > 1:
        half = width // 2
        part = part[half:] + shifted(part[:half], "ctx", -half)
        width = half
    owned = part[0]
    return (
        grad_qlat.astype(jnp.bfloat16),
        grad_qrot.reshape(tok_rows, head_count * rope_width).astype(jnp.bfloat16),
        owned[:, :lat_width].astype(jnp.bfloat16),
        owned[:, lat_width:].astype(jnp.bfloat16),
    )


def solution(mesh):
    in_specs = (
        P("ctx", "head", None),
        P("ctx", "head"),
        P("ctx", "head", None),
        P("ctx", "head", None),
        P("ctx", "head"),
        P("ctx", None),
        P("ctx", None),
        P("ctx"),
    )
    out_specs = (
        P("ctx", "head", None),
        P("ctx", "head"),
        P(("ctx", "head"), None),
        P(("ctx", "head"), None),
    )
    return jax.shard_map(local, mesh=mesh, in_specs=in_specs, out_specs=out_specs, check_vma=False)
```

profile of v0, /device:TPU:69, one launch (start us, length us, event | category | flops | bytes accessed | tf_op | source)
XLA Modules:
  0.0 138.8 jit_solution(6973941782515152101)
XLA Ops:
  0.6 1.0 copy.44
  2.5 4.1 %collective-permute-start = (bf16[1,128,576]{1,2,0:T(8,128)(2,1)S(1)}, bf16[1,128,576]{1,2,0:T(8,128)(2,1)S(1)}, u32[]{:S(2)}, u32[]{:S(2)}) collective-permute-start(bf16[1,128,576]{1,2,0:T(8,128)(2,1)S(1)} %maximum_bitcast_fusion), channel_id=1, source_target_pairs={{0,8},{8,16},{16,24},{24,32},{32,40},{40,48},{48,56},{56,64},{64,7... | collective-permute-start | bytes 442376 | tf_op jit(solution)/shard_map/ppermute | solution.py:14
  6.6 2.1 %collective-permute-done = bf16[1,128,576]{1,2,0:T(8,128)(2,1)S(1)} collective-permute-done((bf16[1,128,576]{1,2,0:T(8,128)(2,1)S(1)}, bf16[1,128,576]{1,2,0:T(8,128)(2,1)S(1)}, u32[]{:S(2)}, u32[]{:S(2)}) %collective-permute-start) | collective-permute-done | bytes 147488 | tf_op jit(solution)/shard_map/ppermute | solution.py:14
  8.7 4.8 %collective-permute-start.1 = (bf16[2,128,576]{1,2,0:T(8,128)(2,1)S(1)}, bf16[2,128,576]{1,2,0:T(8,128)(2,1)S(1)}, u32[]{:S(2)}, u32[]{:S(2)}) collective-permute-start(bf16[2,128,576]{1,2,0:T(8,128)(2,1)S(1)} %pad_maximum_fusion.3), channel_id=1, source_target_pairs={{0,16},{8,24},{16,32},{24,40},{32,48},{40,56},{48,64},{56,72},{64,... | collective-permute-start | bytes 884744 | tf_op jit(solution)/shard_map/ppermute | solution.py:14
  13.5 1.9 %copy.56 = bf16[128,8,512]{0,2,1:T(8,128)(2,1)S(1)} copy(bf16[128,8,512]{2,1,0:T(8,128)(2,1)} %param.11) | data formatting | bytes 2097152 | tf_op args[3]
  15.5 4.6 %collective-permute-done.1 = bf16[2,128,576]{1,2,0:T(8,128)(2,1)S(1)} collective-permute-done((bf16[2,128,576]{1,2,0:T(8,128)(2,1)S(1)}, bf16[2,128,576]{1,2,0:T(8,128)(2,1)S(1)}, u32[]{:S(2)}, u32[]{:S(2)}) %collective-permute-start.1) | collective-permute-done | bytes 294944 | tf_op jit(solution)/shard_map/ppermute | solution.py:14
  20.2 4.4 %collective-permute-start.2 = (bf16[4,128,576]{1,2,0:T(8,128)(2,1)S(1)}, bf16[4,128,576]{1,2,0:T(8,128)(2,1)}, u32[]{:S(2)}, u32[]{:S(2)}) collective-permute-start(bf16[4,128,576]{1,2,0:T(8,128)(2,1)S(1)} %pad_maximum_fusion.2), channel_id=1, source_target_pairs={{0,32},{8,40},{16,48},{24,56},{32,64},{40,72},{48,80},{56,88},{64,... | collective-permute-start | bytes 1769480 | tf_op jit(solution)/shard_map/ppermute | solution.py:14
  24.6 1.6 %fusion.4 = f32[128,8]{1,0:T(8,128)S(1)} fusion(bf16[128,8,512]{2,1,0:T(8,128)(2,1)S(1)} %copy-done.1, bf16[128,8,512]{2,1,0:T(8,128)(2,1)} %param.10), kind=kLoop, calls=%fused_computation.10 | loop fusion | flops 2096128 | bytes 2101248
  27.0 2.7 %copy.54 = bf16[128,8,512]{0,2,1:T(8,128)(2,1)} copy(bf16[128,8,512]{2,1,0:T(8,128)(2,1)} %param.8) | data formatting | bytes 2097152 | tf_op args[0]
  29.7 0.8 compare_and_fusion
  30.5 4.9 %collective-permute-done.2 = bf16[4,128,576]{1,2,0:T(8,128)(2,1)} collective-permute-done((bf16[4,128,576]{1,2,0:T(8,128)(2,1)S(1)}, bf16[4,128,576]{1,2,0:T(8,128)(2,1)}, u32[]{:S(2)}, u32[]{:S(2)}) %collective-permute-start.2) | collective-permute-done | bytes 589856 | tf_op jit(solution)/shard_map/ppermute | solution.py:14
  35.4 1.3 pad_maximum_fusion.1
  37.5 1.7 %fusion.9 = f32[1024,128,8]{1,0,2:T(8,128)S(1)} fusion(bf16[128,8,64]{0,2,1:T(8,128)(2,1)} %bitcast.56, bf16[1024,576]{1,0:T(8,128)(2,1)S(1)} %bitcast.51), kind=kOutput, calls=%fused_computation.24 | convolution fusion | flops 134217728 | bytes 4587520 | tf_op jit(solution)/shard_map/thr,kr->thk/dot_general | solution.py:41
  39.2 1.7 %fusion.3 = f32[128,8,1024]{0,2,1:T(8,128)S(1)} fusion(f32[1024,128,8]{1,0,2:T(8,128)S(1)} %fusion.9, bf16[128,8,512]{0,2,1:T(8,128)(2,1)S(1)} %copy-done.6, f32[128,8]{0,1:T(8,128)S(1)} %copy-done.12, pred[128,1024]{0,1:T(8,128)(4,1)S(1)} %copy-done.10, bf16[1024,576]{1,0:T(8,128)(2,1)S(1)} %bitcast.52), kind=kOutput, calls=%fused_computation.5 | convolution fusion | flops 1078984704 | bytes 10620928 | tf_op jit(solution)/shard_map/thc,kc->thk/dot_general | solution.py:40
  40.9 1.3 fusion.5
  42.2 2.6 %fusion = bf16[128,8,1024]{0,2,1:T(8,128)(2,1)S(1)} fusion(f32[128,8,1024]{0,2,1:T(8,128)S(1)} %fusion.3, bf16[128,8,512]{0,2,1:T(8,128)(2,1)} %copy-done, f32[128,8]{0,1:T(8,128)S(1)} %copy.67, bf16[1024,576]{1,0:T(8,128)(2,1)S(1)} %bitcast.53), kind=kOutput, calls=%fused_computation.1 | convolution fusion | flops 1076887552 | bytes 8392704 | tf_op jit(solution)/shard_map/thc,kc->thk/dot_general | solution.py:46
  45.6 1.3 bitcast_add_fusion
  46.9 1.6 %pad_maximum_fusion = f32[1024,576]{0,1:T(8,128)} fusion(f32[1024,64]{0,1:T(8,128)S(1)} %fusion.7, f32[1024,512]{0,1:T(8,128)S(1)} %bitcast_add_fusion), kind=kLoop, calls=%fused_computation.6 | loop fusion | flops 589824 | bytes 4718592 | tf_op jit(solution)/shard_map/concatenate | solution.py:62
  48.5 3.2 %copy.58 = f32[1024,576]{1,0:T(8,128)} copy(f32[1024,576]{0,1:T(8,128)} %pad_maximum_fusion) | data formatting | bytes 4718592 | tf_op jit(solution)/shard_map/concatenate | solution.py:62
  51.7 2.0 %copy.59 = f32[8,8,16,576]{3,2,0,1:T(8,128)S(1)} copy(f32[8,8,16,576]{3,2,1,0:T(8,128)} %bitcast.50) | data formatting | bytes 4718592 | tf_op jit(solution)/shard_map/reshape | solution.py:64
  53.6 32.7 %all_to_all.5 = f32[8,8,16,576]{3,2,0,1:T(8,128)} all-to-all(f32[8,8,16,576]{3,2,0,1:T(8,128)S(1)} %copy.59), channel_id=1, replica_groups=mesh['ctx'=64,'head'=8] {'head'}, dimensions={1} | all-to-all | bytes 4718592 | tf_op jit(solution)/shard_map/all_to_all | solution.py:65
  86.3 2.6 %reduce_sum.9 = f32[8,16,576]{2,1,0:T(8,128)} reduce(f32[8,8,16,576]{3,2,0,1:T(8,128)} %all_to_all.5, f32[]{:T(128)} %constant.4.clone.1), dimensions={1}, to_apply=%region_0.1 | reduce | flops 516096 | bytes 2654212 | tf_op jit(solution)/shard_map/reduce_sum | solution.py:65
  89.0 0.9 slice.45
  89.9 1.9 %collective-permute-start.3 = (f32[4,16,576]{2,1,0:T(8,128)S(1)}, f32[4,16,576]{2,1,0:T(8,128)S(1)}, u32[]{:S(2)}, u32[]{:S(2)}) collective-permute-start(f32[4,16,576]{2,1,0:T(8,128)S(1)} %slice.45), channel_id=1, source_target_pairs={{32,0},{40,8},{48,16},{56,24},{64,32},{72,40},{80,48},{88,56},{96,... | collective-permute-start | bytes 442376 | tf_op jit(solution)/shard_map/ppermute | solution.py:14
  91.8 23.1 %collective-permute-done.3 = f32[4,16,576]{2,1,0:T(8,128)S(1)} collective-permute-done((f32[4,16,576]{2,1,0:T(8,128)S(1)}, f32[4,16,576]{2,1,0:T(8,128)S(1)}, u32[]{:S(2)}, u32[]{:S(2)}) %collective-permute-start.3) | collective-permute-done | bytes 147488 | tf_op jit(solution)/shard_map/ppermute | solution.py:14
  115.0 0.9 slice_add_fusion
  115.9 7.0 %collective-permute-start.4 = (f32[2,16,576]{2,1,0:T(8,128)S(1)}, f32[2,16,576]{2,1,0:T(8,128)S(1)}, u32[]{:S(2)}, u32[]{:S(2)}) collective-permute-start(f32[2,16,576]{2,1,0:T(8,128)S(1)} %slice.47), channel_id=1, source_target_pairs={{16,0},{24,8},{32,16},{40,24},{48,32},{56,40},{64,48},{72,56},{80,... | collective-permute-start | bytes 221192 | tf_op jit(solution)/shard_map/ppermute | solution.py:14
  122.9 1.3 multiply_convert_fusion
  124.2 2.7 %collective-permute-done.4 = f32[2,16,576]{2,1,0:T(8,128)S(1)} collective-permute-done((f32[2,16,576]{2,1,0:T(8,128)S(1)}, f32[2,16,576]{2,1,0:T(8,128)S(1)}, u32[]{:S(2)}, u32[]{:S(2)}) %collective-permute-start.4) | collective-permute-done | bytes 73760 | tf_op jit(solution)/shard_map/ppermute | solution.py:14
  127.5 4.5 %collective-permute-start.5 = (f32[1,16,576]{2,1,0:T(8,128)}, f32[1,16,576]{2,1,0:T(8,128)}, u32[]{:S(2)}, u32[]{:S(2)}) collective-permute-start(f32[1,16,576]{2,1,0:T(8,128)} %slice.49), channel_id=1, source_target_pairs={{8,0},{16,8},{24,16},{32,24},{40,32},{48,40},{56,48},{64,56},{72,6... | collective-permute-start | bytes 110600 | tf_op jit(solution)/shard_map/ppermute | solution.py:14
  132.6 1.5 %copy.60 = bf16[128,8,512]{2,1,0:T(8,128)(2,1)} copy(bf16[128,8,512]{2,0,1:T(8,128)(2,1)S(1)} %multiply_convert_fusion) | data formatting | bytes 2097152
  134.9 2.0 %collective-permute-done.5 = f32[1,16,576]{2,1,0:T(8,128)} collective-permute-done((f32[1,16,576]{2,1,0:T(8,128)}, f32[1,16,576]{2,1,0:T(8,128)}, u32[]{:S(2)}, u32[]{:S(2)}) %collective-permute-start.5) | collective-permute-done | bytes 36896 | tf_op jit(solution)/shard_map/ppermute | solution.py:14
  (43 shorter events, 7.2 us)
Async XLA Ops:
  1.7 22.9 %copy-start.1 = (bf16[128,8,512]{2,1,0:T(8,128)(2,1)S(1)}, bf16[128,8,512]{2,1,0:T(8,128)(2,1)}, u32[]{:S(2)}) copy-start(bf16[128,8,512]{2,1,0:T(8,128)(2,1)} %param.11) | copy-start | bytes 3145732
  2.5 6.2 %collective-permute-start = (bf16[1,128,576]{1,2,0:T(8,128)(2,1)S(1)}, bf16[1,128,576]{1,2,0:T(8,128)(2,1)S(1)}, u32[]{:S(2)}, u32[]{:S(2)}) collective-permute-start(bf16[1,128,576]{1,2,0:T(8,128)(2,1)S(1)} %maximum_bitcast_fusion), channel_id=1, source_target_pairs={{0,8},{8,16},{16,24},{24,32},{32,40},{40,48},{48,56},{56,64},{64,7... | collective-permute-start | bytes 442376 | tf_op jit(solution)/shard_map/ppermute | solution.py:14
  8.7 17.5 %copy-start.2 = (bf16[1,128,576]{1,2,0:T(8,128)(2,1)}, bf16[1,128,576]{1,2,0:T(8,128)(2,1)S(1)}, u32[]{:S(2)}) copy-start(bf16[1,128,576]{1,2,0:T(8,128)(2,1)S(1)} %collective-permute-done) | copy-start | bytes 442372
  8.7 11.4 %collective-permute-start.1 = (bf16[2,128,576]{1,2,0:T(8,128)(2,1)S(1)}, bf16[2,128,576]{1,2,0:T(8,128)(2,1)S(1)}, u32[]{:S(2)}, u32[]{:S(2)}) collective-permute-start(bf16[2,128,576]{1,2,0:T(8,128)(2,1)S(1)} %pad_maximum_fusion.3), channel_id=1, source_target_pairs={{0,16},{8,24},{16,32},{24,40},{32,48},{40,56},{48,64},{56,72},{64,... | collective-permute-start | bytes 884744 | tf_op jit(solution)/shard_map/ppermute | solution.py:14
  15.4 25.5 %copy-start = (bf16[128,8,512]{0,2,1:T(8,128)(2,1)}, bf16[128,8,512]{0,2,1:T(8,128)(2,1)S(1)}, u32[]{:S(2)}) copy-start(bf16[128,8,512]{0,2,1:T(8,128)(2,1)S(1)} %copy.56) | copy-start | bytes 3145732
  15.5 10.8 %copy-start.9 = (bf16[128,512]{1,0:T(8,128)(2,1)S(1)}, bf16[128,512]{1,0:T(8,128)(2,1)}, u32[]{:S(2)}) copy-start(bf16[128,512]{1,0:T(8,128)(2,1)} %param.9) | copy-start | bytes 393220
  20.1 9.6 %copy-start.4 = (bf16[2,128,576]{1,2,0:T(8,128)(2,1)}, bf16[2,128,576]{1,2,0:T(8,128)(2,1)S(1)}, u32[]{:S(2)}) copy-start(bf16[2,128,576]{1,2,0:T(8,128)(2,1)S(1)} %collective-permute-done.1) | copy-start | bytes 884740
  20.2 9.5 %copy-start.11 = (s32[128]{0:T(128)S(1)}, s32[128]{0:T(128)}, u32[]{:S(2)}) copy-start(s32[128]{0:T(128)} %param.15) | copy-start | bytes 1540
  20.2 15.2 %collective-permute-start.2 = (bf16[4,128,576]{1,2,0:T(8,128)(2,1)S(1)}, bf16[4,128,576]{1,2,0:T(8,128)(2,1)}, u32[]{:S(2)}, u32[]{:S(2)}) collective-permute-start(bf16[4,128,576]{1,2,0:T(8,128)(2,1)S(1)} %pad_maximum_fusion.2), channel_id=1, source_target_pairs={{0,32},{8,40},{16,48},{24,56},{32,64},{40,72},{48,80},{56,88},{64,... | collective-permute-start | bytes 1769480 | tf_op jit(solution)/shard_map/ppermute | solution.py:14
  26.2 9.2 %copy-start.3 = (bf16[1,128,576]{1,2,0:T(8,128)(2,1)S(1)}, bf16[1,128,576]{1,2,0:T(8,128)(2,1)}, u32[]{:S(2)}) copy-start(bf16[1,128,576]{1,2,0:T(8,128)(2,1)} %copy-done.2) | copy-start | bytes 442372
  37.4 1.7 %copy-start.6 = (bf16[128,8,512]{0,2,1:T(8,128)(2,1)S(1)}, bf16[128,8,512]{0,2,1:T(8,128)(2,1)}, u32[]{:S(2)}) copy-start(bf16[128,8,512]{0,2,1:T(8,128)(2,1)} %copy.54) | copy-start | bytes 3145732
  37.5 1.7 %copy-start.10 = (pred[128,1024]{0,1:T(8,128)(4,1)S(1)}, pred[128,1024]{0,1:T(8,128)(4,1)}, u32[]{:S(2)}) copy-start(pred[128,1024]{0,1:T(8,128)(4,1)} %compare_and_fusion) | copy-start | bytes 393220
  37.5 1.7 %copy-start.12 = (f32[128,8]{0,1:T(8,128)S(1)}, f32[128,8]{0,1:T(8,128)}, u32[]{:S(2)}) copy-start(f32[128,8]{0,1:T(8,128)} %param.12) | copy-start | bytes 12292
  42.2 2.6 %copy-start.5 = (bf16[128,512]{0,1:T(8,128)(2,1)S(1)}, bf16[128,512]{0,1:T(8,128)(2,1)}, u32[]{:S(2)}) copy-start(bf16[128,512]{0,1:T(8,128)(2,1)} %copy.47) | copy-start | bytes 393220
  89.9 25.1 %collective-permute-start.3 = (f32[4,16,576]{2,1,0:T(8,128)S(1)}, f32[4,16,576]{2,1,0:T(8,128)S(1)}, u32[]{:S(2)}, u32[]{:S(2)}) collective-permute-start(f32[4,16,576]{2,1,0:T(8,128)S(1)} %slice.45), channel_id=1, source_target_pairs={{32,0},{40,8},{48,16},{56,24},{64,32},{72,40},{80,48},{88,56},{96,... | collective-permute-start | bytes 442376 | tf_op jit(solution)/shard_map/ppermute | solution.py:14
  115.9 11.0 %collective-permute-start.4 = (f32[2,16,576]{2,1,0:T(8,128)S(1)}, f32[2,16,576]{2,1,0:T(8,128)S(1)}, u32[]{:S(2)}, u32[]{:S(2)}) collective-permute-start(f32[2,16,576]{2,1,0:T(8,128)S(1)} %slice.47), channel_id=1, source_target_pairs={{16,0},{24,8},{32,16},{40,24},{48,32},{56,40},{64,48},{72,56},{80,... | collective-permute-start | bytes 221192 | tf_op jit(solution)/shard_map/ppermute | solution.py:14
  126.9 0.6 copy-start.7
  127.5 9.3 %collective-permute-start.5 = (f32[1,16,576]{2,1,0:T(8,128)}, f32[1,16,576]{2,1,0:T(8,128)}, u32[]{:S(2)}, u32[]{:S(2)}) collective-permute-start(f32[1,16,576]{2,1,0:T(8,128)} %slice.49), channel_id=1, source_target_pairs={{8,0},{16,8},{24,16},{32,24},{40,32},{48,40},{56,48},{64,56},{72,6... | collective-permute-start | bytes 110600 | tf_op jit(solution)/shard_map/ppermute | solution.py:14
  132.6 4.3 %copy-start.8 = (f32[2,16,576]{2,1,0:T(8,128)S(1)}, f32[2,16,576]{2,1,0:T(8,128)}, u32[]{:S(2)}) copy-start(f32[2,16,576]{2,1,0:T(8,128)} %copy-done.7) | copy-start | bytes 221188
where the time goes:
time: 140 us; the launch traced here: 139 us
  waiting for transfers between devices  39.3 us (28%)
  blocking collectives  32.7 us (23%)
  starting transfers between devices  26.7 us (19%)
  local copies, waits for them, and re-layouts  17.5 us (12%)
  matrix products  11.1 us (8%)
  other arithmetic  10.7 us (8%)
    ppermute x6, waiting for transfers between devices, shifted(): return lax.ppermute(x, axis, pairs)  39.3 us
    all_to_all x1, blocking collectives, local(): part = lax.all_to_all(part, 'head', 1, 1, tiled=True).sum(axis=1)  32.7 us
    ppermute x6, starting transfers between devices, shifted(): return lax.ppermute(x, axis, pairs)  26.7 us
    unnamed x32, local copies, waits for them, and re-layouts  8.78 us
    concatenate x1, local copies, waits for them, and re-layouts, local(): part = jnp.concatenate([grad_lat, grad_rot], axis=1)  3.18 us
  transfers between devices with their start and end apart: 6, of which 6 were waited for; matrix products, arithmetic and copies ran while one was open for 9% of the time, Pallas kernels for 0%

commit v1 on v0

--- a/solution.py
+++ b/solution.py
@@ -6,6 +6,12 @@
 ROPE = 64
 NOPE = 128
 LEVELS = 3
+
+
+def trade_parts(x, axis, split, join):
+    pieces = jnp.split(x, lax.axis_size(axis), axis=split)
+    received = lax.all_to_all(jnp.stack(pieces), axis, 0, 0)
+    return jnp.concatenate(received, axis=join)
 
 
 def shifted(x, axis, by):
@@ -62,7 +68,7 @@
     part = jnp.concatenate([grad_lat, grad_rot], axis=1)
     block = tok_rows // groups
     part = part.reshape(span, groups, block, lat_width + rope_width)
-    part = lax.all_to_all(part, "head", 1, 1, tiled=True).sum(axis=1)
+    part = trade_parts(part, "head", 1, 1).sum(axis=1)
     width = span
     while width > 1:
         half = width // 2

time: 140 us -> 142 us (1.014)
  local copies, waits for them, and re-layouts: 17.5 us -> 19.9 us
    unnamed x32 -> x37, local copies, waits for them, and re-layouts: 8.78 us -> 13.1 us
    reshape x1 -> x0, local copies, waits for them, and re-layouts: 1.98 us -> none  [local(): part = part.reshape(span, groups, block, lat_width + rope_width)]
where the time goes in v1:
time: 142 us; the launch traced here: 141 us
  waiting for transfers between devices  39.3 us (28%)
  blocking collectives  32.7 us (23%)
  starting transfers between devices  26.5 us (19%)
  local copies, waits for them, and re-layouts  19.9 us (14%)
  matrix products  11.1 us (8%)
  other arithmetic  10.7 us (8%)
    ppermute x6, waiting for transfers between devices, shifted(): return lax.ppermute(x, axis, pairs)  39.3 us
    all_to_all x1, blocking collectives, trade_parts(): received = lax.all_to_all(jnp.stack(pieces), axis, 0, 0)  32.7 us
    ppermute x6, starting transfers between devices, shifted(): return lax.ppermute(x, axis, pairs)  26.5 us
    unnamed x37, local copies, waits for them, and re-layouts  13.1 us
    concatenate x1, local copies, waits for them, and re-layouts, local(): part = jnp.concatenate([grad_lat, grad_rot], axis=1)  3.19 us
  transfers between devices with their start and end apart: 6, of which 6 were waited for; matrix products, arithmetic and copies ran while one was open for 9% of the time, Pallas kernels for 0%

profile of v1, /device:TPU:69, one launch (start us, length us, event | category | flops | bytes accessed | tf_op | source)
XLA Modules:
  0.0 141.1 jit_solution(17706311028627163974)
XLA Ops:
  0.6 1.1 copy.58
  2.5 4.1 %collective-permute-start = (bf16[1,128,576]{1,2,0:T(8,128)(2,1)S(1)}, bf16[1,128,576]{1,2,0:T(8,128)(2,1)S(1)}, u32[]{:S(2)}, u32[]{:S(2)}) collective-permute-start(bf16[1,128,576]{1,2,0:T(8,128)(2,1)S(1)} %maximum_bitcast_fusion), channel_id=1, source_target_pairs={{0,8},{8,16},{16,24},{24,32},{32,40},{40,48},{48,56},{56,64},{64,7... | collective-permute-start | bytes 442376 | tf_op jit(solution)/shard_map/ppermute | solution.py:20
  6.6 2.1 %collective-permute-done = bf16[1,128,576]{1,2,0:T(8,128)(2,1)S(1)} collective-permute-done((bf16[1,128,576]{1,2,0:T(8,128)(2,1)S(1)}, bf16[1,128,576]{1,2,0:T(8,128)(2,1)S(1)}, u32[]{:S(2)}, u32[]{:S(2)}) %collective-permute-start) | collective-permute-done | bytes 147488 | tf_op jit(solution)/shard_map/ppermute | solution.py:20
  8.7 4.8 %collective-permute-start.1 = (bf16[2,128,576]{1,2,0:T(8,128)(2,1)S(1)}, bf16[2,128,576]{1,2,0:T(8,128)(2,1)S(1)}, u32[]{:S(2)}, u32[]{:S(2)}) collective-permute-start(bf16[2,128,576]{1,2,0:T(8,128)(2,1)S(1)} %pad_maximum_fusion.3), channel_id=1, source_target_pairs={{0,16},{8,24},{16,32},{24,40},{32,48},{40,56},{48,64},{56,72},{64,... | collective-permute-start | bytes 884744 | tf_op jit(solution)/shard_map/ppermute | solution.py:20
  13.5 2.0 %copy.70 = bf16[128,8,512]{0,2,1:T(8,128)(2,1)S(1)} copy(bf16[128,8,512]{2,1,0:T(8,128)(2,1)} %param.11) | data formatting | bytes 2097152 | tf_op args[3]
  15.5 4.6 %collective-permute-done.1 = bf16[2,128,576]{1,2,0:T(8,128)(2,1)S(1)} collective-permute-done((bf16[2,128,576]{1,2,0:T(8,128)(2,1)S(1)}, bf16[2,128,576]{1,2,0:T(8,128)(2,1)S(1)}, u32[]{:S(2)}, u32[]{:S(2)}) %collective-permute-start.1) | collective-permute-done | bytes 294944 | tf_op jit(solution)/shard_map/ppermute | solution.py:20
  20.2 4.3 %collective-permute-start.2 = (bf16[4,128,576]{1,2,0:T(8,128)(2,1)S(1)}, bf16[4,128,576]{1,2,0:T(8,128)(2,1)}, u32[]{:S(2)}, u32[]{:S(2)}) collective-permute-start(bf16[4,128,576]{1,2,0:T(8,128)(2,1)S(1)} %pad_maximum_fusion.2), channel_id=1, source_target_pairs={{0,32},{8,40},{16,48},{24,56},{32,64},{40,72},{48,80},{56,88},{64,... | collective-permute-start | bytes 1769480 | tf_op jit(solution)/shard_map/ppermute | solution.py:20
  24.4 1.6 %fusion.4 = f32[128,8]{1,0:T(8,128)S(1)} fusion(bf16[128,8,512]{2,1,0:T(8,128)(2,1)S(1)} %copy-done.2, bf16[128,8,512]{2,1,0:T(8,128)(2,1)} %param.10), kind=kLoop, calls=%fused_computation.10 | loop fusion | flops 2096128 | bytes 2101248
  26.9 2.7 %copy.68 = bf16[128,8,512]{0,2,1:T(8,128)(2,1)} copy(bf16[128,8,512]{2,1,0:T(8,128)(2,1)} %param.8) | data formatting | bytes 2097152 | tf_op args[0]
  30.4 5.0 %collective-permute-done.2 = bf16[4,128,576]{1,2,0:T(8,128)(2,1)} collective-permute-done((bf16[4,128,576]{1,2,0:T(8,128)(2,1)S(1)}, bf16[4,128,576]{1,2,0:T(8,128)(2,1)}, u32[]{:S(2)}, u32[]{:S(2)}) %collective-permute-start.2) | collective-permute-done | bytes 589856 | tf_op jit(solution)/shard_map/ppermute | solution.py:20
  35.4 1.4 %pad_maximum_fusion.1 = bf16[8,128,576]{1,2,0:T(8,128)(2,1)S(1)} fusion(bf16[1,128,576]{1,2,0:T(8,128)(2,1)S(1)} %maximum_bitcast_fusion, bf16[1,128,576]{1,2,0:T(8,128)(2,1)} %copy-done.3, bf16[2,128,576]{1,2,0:T(8,128)(2,1)} %copy-done.4, bf16[4,128,576]{1,2,0:T(8,128)(2,1)} %collective-permute-done.2), kind=kLoop, calls=%fused_computation.14 | loop fusion | flops 1769472 | bytes 2359296 | tf_op jit(solution)/shard_map/concatenate | solution.py:36
  37.6 1.7 %fusion.17 = f32[1024,128,8]{1,0,2:T(8,128)S(1)} fusion(bf16[128,8,64]{0,2,1:T(8,128)(2,1)} %bitcast.109, bf16[1024,576]{1,0:T(8,128)(2,1)S(1)} %bitcast.104), kind=kOutput, calls=%fused_computation.40 | convolution fusion | flops 134217728 | bytes 4587520 | tf_op jit(solution)/shard_map/thr,kr->thk/dot_general | solution.py:47
  39.3 1.7 %fusion.3 = f32[128,8,1024]{0,2,1:T(8,128)S(1)} fusion(f32[1024,128,8]{1,0,2:T(8,128)S(1)} %fusion.17, bf16[128,8,512]{0,2,1:T(8,128)(2,1)S(1)} %copy-done.6, f32[128,8]{0,1:T(8,128)S(1)} %copy-done.11, pred[128,1024]{0,1:T(8,128)(4,1)S(1)} %copy-done.9, bf16[1024,576]{1,0:T(8,128)(2,1)S(1)} %bitcast.105), kind=kOutput, calls=%fused_computation.5 | convolution fusion | flops 1078984704 | bytes 10620928 | tf_op jit(solution)/shard_map/thc,kc->thk/dot_general | solution.py:46
  41.0 1.3 fusion.5
  42.3 2.6 %fusion = bf16[128,8,1024]{0,2,1:T(8,128)(2,1)S(1)} fusion(f32[128,8,1024]{0,2,1:T(8,128)S(1)} %fusion.3, bf16[128,8,512]{0,2,1:T(8,128)(2,1)} %copy-done.1, f32[128,8]{0,1:T(8,128)S(1)} %copy.87, bf16[1024,576]{1,0:T(8,128)(2,1)S(1)} %bitcast.106), kind=kOutput, calls=%fused_computation.1 | convolution fusion | flops 1076887552 | bytes 8392704 | tf_op jit(solution)/shard_map/thc,kc->thk/dot_general | solution.py:52
  45.7 1.3 bitcast_add_fusion
  47.0 1.6 %pad_maximum_fusion = f32[1024,576]{0,1:T(8,128)} fusion(f32[1024,64]{0,1:T(8,128)S(1)} %fusion.7, f32[1024,512]{0,1:T(8,128)S(1)} %bitcast_add_fusion), kind=kLoop, calls=%fused_computation.6 | loop fusion | flops 589824 | bytes 4718592 | tf_op jit(solution)/shard_map/concatenate | solution.py:68
  48.6 3.2 %copy.72 = f32[1024,576]{1,0:T(8,128)} copy(f32[1024,576]{0,1:T(8,128)} %pad_maximum_fusion) | data formatting | bytes 4718592 | tf_op jit(solution)/shard_map/concatenate | solution.py:68
  51.8 1.1 fusion.16
  52.9 1.0 fusion.15
  53.9 1.0 fusion.14
  54.9 1.0 fusion.13
  56.1 32.7 %all_to_all.5 = f32[8,8,1,16,576]{4,3,1,2,0:T(8,128)} all-to-all(f32[8,8,1,16,576]{4,3,1,2,0:T(8,128)S(1)} %fusion.9), channel_id=1, replica_groups=mesh['ctx'=64,'head'=8] {'head'}, dimensions={0} | all-to-all | bytes 4718592 | tf_op jit(solution)/shard_map/all_to_all | solution.py:13
  88.7 2.6 %reduce_sum.9 = f32[8,16,576]{2,1,0:T(8,128)} reduce(f32[8,8,1,16,576]{4,3,1,2,0:T(8,128)} %all_to_all.5, f32[]{:T(128)} %constant.4.clone.1), dimensions={0,2}, to_apply=%region_0.1 | reduce | flops 516096 | bytes 2654212 | tf_op jit(solution)/shard_map/reduce_sum | solution.py:71
  92.3 1.9 %collective-permute-start.3 = (f32[4,16,576]{2,1,0:T(8,128)S(1)}, f32[4,16,576]{2,1,0:T(8,128)S(1)}, u32[]{:S(2)}, u32[]{:S(2)}) collective-permute-start(f32[4,16,576]{2,1,0:T(8,128)S(1)} %slice.45), channel_id=1, source_target_pairs={{32,0},{40,8},{48,16},{56,24},{64,32},{72,40},{80,48},{88,56},{96,... | collective-permute-start | bytes 442376 | tf_op jit(solution)/shard_map/ppermute | solution.py:20
  94.2 23.0 %collective-permute-done.3 = f32[4,16,576]{2,1,0:T(8,128)S(1)} collective-permute-done((f32[4,16,576]{2,1,0:T(8,128)S(1)}, f32[4,16,576]{2,1,0:T(8,128)S(1)}, u32[]{:S(2)}, u32[]{:S(2)}) %collective-permute-start.3) | collective-permute-done | bytes 147488 | tf_op jit(solution)/shard_map/ppermute | solution.py:20
  118.2 7.0 %collective-permute-start.4 = (f32[2,16,576]{2,1,0:T(8,128)S(1)}, f32[2,16,576]{2,1,0:T(8,128)S(1)}, u32[]{:S(2)}, u32[]{:S(2)}) collective-permute-start(f32[2,16,576]{2,1,0:T(8,128)S(1)} %slice.47), channel_id=1, source_target_pairs={{16,0},{24,8},{32,16},{40,24},{48,32},{56,40},{64,48},{72,56},{80,... | collective-permute-start | bytes 221192 | tf_op jit(solution)/shard_map/ppermute | solution.py:20
  125.2 1.3 multiply_convert_fusion
  126.5 2.7 %collective-permute-done.4 = f32[2,16,576]{2,1,0:T(8,128)S(1)} collective-permute-done((f32[2,16,576]{2,1,0:T(8,128)S(1)}, f32[2,16,576]{2,1,0:T(8,128)S(1)}, u32[]{:S(2)}, u32[]{:S(2)}) %collective-permute-start.4) | collective-permute-done | bytes 73760 | tf_op jit(solution)/shard_map/ppermute | solution.py:20
  129.8 4.5 %collective-permute-start.5 = (f32[1,16,576]{2,1,0:T(8,128)}, f32[1,16,576]{2,1,0:T(8,128)}, u32[]{:S(2)}, u32[]{:S(2)}) collective-permute-start(f32[1,16,576]{2,1,0:T(8,128)} %slice.49), channel_id=1, source_target_pairs={{8,0},{16,8},{24,16},{32,24},{40,32},{48,40},{56,48},{64,56},{72,6... | collective-permute-start | bytes 110600 | tf_op jit(solution)/shard_map/ppermute | solution.py:20
  134.8 1.5 %copy.80 = bf16[128,8,512]{2,1,0:T(8,128)(2,1)} copy(bf16[128,8,512]{2,0,1:T(8,128)(2,1)S(1)} %multiply_convert_fusion) | data formatting | bytes 2097152
  137.2 2.0 %collective-permute-done.5 = f32[1,16,576]{2,1,0:T(8,128)} collective-permute-done((f32[1,16,576]{2,1,0:T(8,128)}, f32[1,16,576]{2,1,0:T(8,128)}, u32[]{:S(2)}, u32[]{:S(2)}) %collective-permute-start.5) | collective-permute-done | bytes 36896 | tf_op jit(solution)/shard_map/ppermute | solution.py:20
  (48 shorter events, 10.0 us)
Async XLA Ops:
  0.6 23.8 %copy-start.2 = (bf16[128,8,512]{2,1,0:T(8,128)(2,1)S(1)}, bf16[128,8,512]{2,1,0:T(8,128)(2,1)}, u32[]{:S(2)}) copy-start(bf16[128,8,512]{2,1,0:T(8,128)(2,1)} %param.11) | copy-start | bytes 3145732
  2.5 6.2 %collective-permute-start = (bf16[1,128,576]{1,2,0:T(8,128)(2,1)S(1)}, bf16[1,128,576]{1,2,0:T(8,128)(2,1)S(1)}, u32[]{:S(2)}, u32[]{:S(2)}) collective-permute-start(bf16[1,128,576]{1,2,0:T(8,128)(2,1)S(1)} %maximum_bitcast_fusion), channel_id=1, source_target_pairs={{0,8},{8,16},{16,24},{24,32},{32,40},{40,48},{48,56},{56,64},{64,7... | collective-permute-start | bytes 442376 | tf_op jit(solution)/shard_map/ppermute | solution.py:20
  8.7 17.3 %copy-start.3 = (bf16[1,128,576]{1,2,0:T(8,128)(2,1)}, bf16[1,128,576]{1,2,0:T(8,128)(2,1)S(1)}, u32[]{:S(2)}) copy-start(bf16[1,128,576]{1,2,0:T(8,128)(2,1)S(1)} %collective-permute-done) | copy-start | bytes 442372
  8.7 11.4 %collective-permute-start.1 = (bf16[2,128,576]{1,2,0:T(8,128)(2,1)S(1)}, bf16[2,128,576]{1,2,0:T(8,128)(2,1)S(1)}, u32[]{:S(2)}, u32[]{:S(2)}) collective-permute-start(bf16[2,128,576]{1,2,0:T(8,128)(2,1)S(1)} %pad_maximum_fusion.3), channel_id=1, source_target_pairs={{0,16},{8,24},{16,32},{24,40},{32,48},{40,56},{48,64},{56,72},{64,... | collective-permute-start | bytes 884744 | tf_op jit(solution)/shard_map/ppermute | solution.py:20
  13.5 12.6 %copy-start.8 = (bf16[128,512]{1,0:T(8,128)(2,1)S(1)}, bf16[128,512]{1,0:T(8,128)(2,1)}, u32[]{:S(2)}) copy-start(bf16[128,512]{1,0:T(8,128)(2,1)} %param.9) | copy-start | bytes 393220
  15.5 25.5 %copy-start.1 = (bf16[128,8,512]{0,2,1:T(8,128)(2,1)}, bf16[128,8,512]{0,2,1:T(8,128)(2,1)S(1)}, u32[]{:S(2)}) copy-start(bf16[128,8,512]{0,2,1:T(8,128)(2,1)S(1)} %copy.70) | copy-start | bytes 3145732
  15.5 14.0 %copy-start.10 = (s32[128]{0:T(128)S(1)}, s32[128]{0:T(128)}, u32[]{:S(2)}) copy-start(s32[128]{0:T(128)} %param.15) | copy-start | bytes 1540
  20.1 9.4 %copy-start.4 = (bf16[2,128,576]{1,2,0:T(8,128)(2,1)}, bf16[2,128,576]{1,2,0:T(8,128)(2,1)S(1)}, u32[]{:S(2)}) copy-start(bf16[2,128,576]{1,2,0:T(8,128)(2,1)S(1)} %collective-permute-done.1) | copy-start | bytes 884740
  20.2 15.2 %collective-permute-start.2 = (bf16[4,128,576]{1,2,0:T(8,128)(2,1)S(1)}, bf16[4,128,576]{1,2,0:T(8,128)(2,1)}, u32[]{:S(2)}, u32[]{:S(2)}) collective-permute-start(bf16[4,128,576]{1,2,0:T(8,128)(2,1)S(1)} %pad_maximum_fusion.2), channel_id=1, source_target_pairs={{0,32},{8,40},{16,48},{24,56},{32,64},{40,72},{48,80},{56,88},{64,... | collective-permute-start | bytes 1769480 | tf_op jit(solution)/shard_map/ppermute | solution.py:20
  37.5 1.7 %copy-start.6 = (bf16[128,8,512]{0,2,1:T(8,128)(2,1)S(1)}, bf16[128,8,512]{0,2,1:T(8,128)(2,1)}, u32[]{:S(2)}) copy-start(bf16[128,8,512]{0,2,1:T(8,128)(2,1)} %copy.68) | copy-start | bytes 3145732
  37.5 1.7 %copy-start.9 = (pred[128,1024]{0,1:T(8,128)(4,1)S(1)}, pred[128,1024]{0,1:T(8,128)(4,1)}, u32[]{:S(2)}) copy-start(pred[128,1024]{0,1:T(8,128)(4,1)} %compare_and_fusion) | copy-start | bytes 393220
  37.6 1.7 %copy-start.11 = (f32[128,8]{0,1:T(8,128)S(1)}, f32[128,8]{0,1:T(8,128)}, u32[]{:S(2)}) copy-start(f32[128,8]{0,1:T(8,128)} %param.12) | copy-start | bytes 12292
  42.3 2.6 %copy-start.5 = (bf16[128,512]{0,1:T(8,128)(2,1)S(1)}, bf16[128,512]{0,1:T(8,128)(2,1)}, u32[]{:S(2)}) copy-start(bf16[128,512]{0,1:T(8,128)(2,1)} %copy.61) | copy-start | bytes 393220
  51.8 4.2 %copy-start = (f32[1024,576]{1,0:T(8,128)S(1)}, f32[1024,576]{1,0:T(8,128)}, u32[]{:S(2)}) copy-start(f32[1024,576]{1,0:T(8,128)} %copy.72) | copy-start | bytes 7077892
  92.3 24.9 %collective-permute-start.3 = (f32[4,16,576]{2,1,0:T(8,128)S(1)}, f32[4,16,576]{2,1,0:T(8,128)S(1)}, u32[]{:S(2)}, u32[]{:S(2)}) collective-permute-start(f32[4,16,576]{2,1,0:T(8,128)S(1)} %slice.45), channel_id=1, source_target_pairs={{32,0},{40,8},{48,16},{56,24},{64,32},{72,40},{80,48},{88,56},{96,... | collective-permute-start | bytes 442376 | tf_op jit(solution)/shard_map/ppermute | solution.py:20
  118.2 11.0 %collective-permute-start.4 = (f32[2,16,576]{2,1,0:T(8,128)S(1)}, f32[2,16,576]{2,1,0:T(8,128)S(1)}, u32[]{:S(2)}, u32[]{:S(2)}) collective-permute-start(f32[2,16,576]{2,1,0:T(8,128)S(1)} %slice.47), channel_id=1, source_target_pairs={{16,0},{24,8},{32,16},{40,24},{48,32},{56,40},{64,48},{72,56},{80,... | collective-permute-start | bytes 221192 | tf_op jit(solution)/shard_map/ppermute | solution.py:20
  129.2 0.7 copy-start.7
  129.8 9.3 %collective-permute-start.5 = (f32[1,16,576]{2,1,0:T(8,128)}, f32[1,16,576]{2,1,0:T(8,128)}, u32[]{:S(2)}, u32[]{:S(2)}) collective-permute-start(f32[1,16,576]{2,1,0:T(8,128)} %slice.49), channel_id=1, source_target_pairs={{8,0},{16,8},{24,16},{32,24},{40,32},{48,40},{56,48},{64,56},{72,6... | collective-permute-start | bytes 110600 | tf_op jit(solution)/shard_map/ppermute | solution.py:20
